TPU v7x, 512 devices: a whole 4x8x8 slice. The times are simulated.
512 devices in a mesh: dp: 32 (over y, x), tensor: 16 (over z, core).
Axes of the slice: x: 4, y: 8, z: 8, core: 2. Of those that a mesh axis runs over, the one named last changes fastest.
Arguments:
- patch_rows: bfloat16 [32, 3072, 1792], P('dp', 'tensor'), may hold values from -6 to 6
- send_rows: int32 [32, 16, 32, 6], P('dp', 'tensor'), may hold values from 0 to 192, as said below
- take_rows: int32 [32, 2048], P('dp', 'tensor'), may hold values from 0 to 191, as said below
- segments: int32 [32, 2048], P('dp', 'tensor'), may hold values from 0 to 41, never falling along the last dimension, each value on 1 to 96 neighbouring positions
- norm_gain: float32 [1792], replicated, may hold values from 0.5 to 5
- qkv_weight: bfloat16 [1792, 2688], P('tensor'), may hold values from -0.125 to 0.125
- out_weight: bfloat16 [896, 1792], P('tensor'), may hold values from -0.1875 to 0.1875
- grad_out: bfloat16 [32, 2048, 1792], P('dp', 'tensor'), may hold values from -6 to 6
Outputs:
- layer_out: bfloat16 [32, 2048, 1792], P('dp', 'tensor')
- patch_grad: bfloat16 [32, 3072, 1792], P('dp', 'tensor')
Inputs may be any that keep to these rules, and one draw needn't show every extreme that they name: `send_rows`: for each source device (s, t) the entries below 192 are distinct, 128 in all; for each group they fill slots from 0 on, the rest being 192; some device sends 6 rows to some group. `take_rows`: for each g and t the 128 entries are distinct and name exactly the slots s * 6 + c that hold a row (c below the number of rows that device (s, t) sends to group g). `segments`: along each row the ids never fall and each id covers 1 to 96 positions.
All inputs are finite; a program needn't handle non-finite values.
Results may differ from a plain program's by a relative error of at most 0.009.
The roundings to bfloat16 on the way count: a program that leaves them out, or rounds other values in their place, can miss the bound.
Values may be sent and summed in bfloat16 or wider, within the bound.
No kernel may reach another device: no remote copies, remote signals or barrier semaphores. Data moves between devices by JAX's collectives and lax.ppermute only.
A program may use at most 128 MiB of HBM per device.

v0:
```python
import jax
import jax.numpy as jnp
from jax import lax
from jax.sharding import PartitionSpec as P

HD = 112
HEADS = 8
MOST = 96


def extended(block, sides, width):
    for axis, dim in sides:
        count = lax.axis_size(axis)
        forward = [(i, i + 1) for i in range(count - 1)]
        backward = [(target, source) for source, target in forward]
        low = lax.ppermute(
            lax.slice_in_dim(block, block.shape[dim] - width, None, axis=dim), axis, forward
        )
        high = lax.ppermute(lax.slice_in_dim(block, 0, width, axis=dim), axis, backward)
        block = jnp.concatenate([low, block, high], axis=dim)
    return block


def normalize(rows_in, norm_gain):
    values = rows_in.astype(jnp.float32)
    center = values - jnp.mean(values, axis=-1, keepdims=True)
    inv_dev = lax.rsqrt(jnp.mean(center * center, axis=-1, keepdims=True) + 1e-06)
    unit_rows = center * inv_dev
    return (values, unit_rows, inv_dev, (unit_rows * norm_gain).astype(jnp.bfloat16))


def split_heads(rows_in):
    return rows_in.reshape(rows_in.shape[0], HEADS, HD)


def attend(queries, keyval, seg_query, seg_key):
    all_heads = HEADS * HD
    score_scale = HD ** (-0.5)
    query_heads = split_heads(queries)
    key_heads = split_heads(keyval[:, :all_heads])
    value_heads = split_heads(keyval[:, all_heads:])
    scores = (
        jnp.einsum("qhd,khd->hqk", query_heads, key_heads, preferred_element_type=jnp.float32)
        * score_scale
    )
    same_chart = seg_query[:, None] == seg_key[None, :]
    scores = jnp.where(same_chart[None], scores, -jnp.inf)
    row_max = jnp.max(scores, axis=2, keepdims=True)
    exp_scores = jnp.exp(scores - row_max)
    row_sum = jnp.sum(exp_scores, axis=2, keepdims=True)
    attn_probs = exp_scores / row_sum
    prob_low = attn_probs.astype(jnp.bfloat16)
    attended = jnp.einsum("hqk,khd->qhd", prob_low, value_heads, preferred_element_type=jnp.float32)
    return (
        attn_probs,
        prob_low,
        attended.astype(jnp.bfloat16).reshape(queries.shape[0], all_heads),
        row_max + jnp.log(row_sum),
    )


def local(patch_rows, send_rows, take_rows, segments, norm_gain, qkv_weight, out_weight, grad_out):
    groups = lax.axis_size("dp")
    src_count = patch_rows.shape[1]
    features = patch_rows.shape[2]
    slot_count = send_rows.shape[3]
    own_rows = take_rows.shape[1]
    all_heads = HEADS * HD
    score_scale = HD ** (-0.5)
    patches = patch_rows[0]
    send_flat = send_rows.reshape(groups * slot_count)
    outgoing = jnp.take(patches, send_flat, axis=0, mode="fill", fill_value=0).reshape(
        groups, slot_count, features
    )
    incoming = lax.all_to_all(outgoing, "dp", split_axis=0, concat_axis=0, tiled=True).reshape(
        groups * slot_count, features
    )
    pick_rows = take_rows[0]
    packed = jnp.take(incoming, pick_rows, axis=0)
    full_qkv, full_out = (
        lax.all_gather(qkv_weight, "tensor", axis=0, tiled=True),
        lax.all_gather(out_weight, "tensor", axis=0, tiled=True),
    )
    values, unit_rows, inv_dev, normed = normalize(packed, norm_gain)
    projected = jnp.dot(normed, full_qkv, preferred_element_type=jnp.float32).astype(jnp.bfloat16)
    queries = projected[:, :all_heads]
    keyval = projected[:, all_heads:]
    seg_plus = segments[0] + 1
    wide_kv, wide_seg = (
        extended(keyval, (("tensor", 0),), MOST),
        extended(seg_plus, (("tensor", 0),), MOST),
    )
    attn_probs, prob_low, attended, log_norm = attend(queries, wide_kv, seg_plus, wide_seg)
    layer_out = (values + jnp.dot(attended, full_out, preferred_element_type=jnp.float32)).astype(
        jnp.bfloat16
    )
    grad_rows = grad_out[0]
    grad_att = lax.dot_general(
        grad_rows, full_out, (((1,), (1,)), ((), ())), preferred_element_type=jnp.float32
    ).astype(jnp.bfloat16)
    query_heads = split_heads(queries)
    grad_heads = split_heads(grad_att)
    wide_keys = split_heads(wide_kv[:, :all_heads])
    wide_values = split_heads(wide_kv[:, all_heads:])
    dprobs = jnp.einsum("qhd,khd->hqk", grad_heads, wide_values, preferred_element_type=jnp.float32)
    row_inner = jnp.sum(attn_probs * dprobs, axis=2, keepdims=True)
    dscore = (attn_probs * (dprobs - row_inner) * score_scale).astype(jnp.bfloat16)
    grad_query = jnp.einsum(
        "hqk,khd->qhd", dscore, wide_keys, preferred_element_type=jnp.float32
    ).reshape(own_rows, all_heads)
    window_rows = wide_kv.shape[0]
    grad_key = jnp.einsum("hqk,qhd->khd", dscore, query_heads, preferred_element_type=jnp.float32)
    grad_value = jnp.einsum(
        "hqk,qhd->khd", prob_low, grad_heads, preferred_element_type=jnp.float32
    )
    grad_window = jnp.concatenate(
        [grad_key.reshape(window_rows, all_heads), grad_value.reshape(window_rows, all_heads)],
        axis=1,
    )
    center = grad_window[MOST : MOST + own_rows]
    rim_parts = jnp.concatenate([grad_window[:MOST], grad_window[MOST + own_rows :]], axis=0)
    arrived = extended(rim_parts, (("tensor", 0),), MOST)
    center = center.at[:MOST].add(arrived[:MOST])
    center = center.at[own_rows - MOST :].add(arrived[3 * MOST :])
    grad_proj = jnp.concatenate([grad_query, center], axis=1).astype(jnp.bfloat16)
    grad_normed = lax.dot_general(
        grad_proj, full_qkv, (((1,), (1,)), ((), ())), preferred_element_type=jnp.float32
    )
    scaled = grad_normed * norm_gain
    grad_unit = (
        scaled
        - jnp.mean(scaled, axis=-1, keepdims=True)
        - unit_rows * jnp.mean(scaled * unit_rows, axis=-1, keepdims=True)
    )
    grad_packed = (grad_rows.astype(jnp.float32) + inv_dev * grad_unit).astype(jnp.bfloat16)
    back_slots = (
        jnp.zeros((groups * slot_count, features), jnp.bfloat16).at[pick_rows].set(grad_packed)
    )
    back_slots = back_slots.reshape(groups, slot_count, features)
    returned = lax.all_to_all(back_slots, "dp", split_axis=0, concat_axis=0, tiled=True).reshape(
        groups * slot_count, features
    )
    patch_grad = (
        jnp.zeros((src_count + 1, features), jnp.bfloat16).at[send_flat].add(returned)[:src_count]
    )
    return (layer_out[None], patch_grad[None])


def solution(mesh):
    return jax.shard_map(
        local,
        mesh=mesh,
        in_specs=(
            P("dp", "tensor", None),
            P("dp", "tensor", None, None),
            P("dp", "tensor"),
            P("dp", "tensor"),
            P(),
            P("tensor", None),
            P("tensor", None),
            P("dp", "tensor", None),
        ),
        out_specs=(P("dp", "tensor", None), P("dp", "tensor", None)),
        check_vma=False,
    )
```

profile of v0, /device:TPU:1, one launch (start us, length us, event | category | flops | bytes accessed | tf_op | source)
XLA Modules:
  0.0 227.3 jit_solution(14492804435034020752)
XLA Ops:
  7.2 0.7 all-gather.3.cloned.1.call-update
  8.0 0.7 all-gather.5.cloned.1.call-update
  8.7 0.8 copy.21
  9.4 0.7 compare_and_fusion
  10.1 0.1 copy.20
  10.2 0.1 reshape.254
  10.4 1.1 gather_fusion
  11.5 0.2 gather.11
  11.7 1.2 broadcast_select_fusion
  12.9 10.6 %all-to-all-start = ((bf16[32,6,1792]{2,1,0:T(8,128)(2,1)}), bf16[32,6,1792]{2,1,0:T(8,128)(2,1)S(1)}, u32[]{:S(2)}, u32[]{:S(2)}) async-start(bf16[32,6,1792]{2,1,0:T(8,128)(2,1)} %broadcast_select_fusion), calls=%async_computation | async-start | bytes 1835008 | tf_op jit(solution)/shard_map/all_to_all | solution.py:75
  23.6 4.8 %collective-permute-start.2 = (s32[96]{0:T(128)S(1)}, s32[96]{0:T(128)S(1)}, u32[]{:S(2)}, u32[]{:S(2)}) collective-permute-start(s32[96]{0:T(128)S(1)} %get-tuple-element.36), channel_id=1, source_target_pairs={{0,1},{1,2},{2,3},{3,4},{4,5},{5,6},{6,7},{7,8},{8,9},{9,10},{10,1... | collective-permute-start | bytes 1160 | tf_op jit(solution)/shard_map/ppermute | solution.py:16
  28.5 1.9 collective-permute-start.3
  30.5 3.3 %collective-permute-done.3 = s32[96]{0:T(128)S(1)} collective-permute-done((s32[96]{0:T(128)S(1)}, s32[96]{0:T(128)S(1)}, u32[]{:S(2)}, u32[]{:S(2)}) %collective-permute-start.3) | collective-permute-done | bytes 416 | tf_op jit(solution)/shard_map/ppermute | solution.py:19
  33.7 0.1 pad_add_fusion
  33.8 13.2 %all-to-all-done = bf16[32,6,1792]{2,1,0:T(8,128)(2,1)S(1)} async-done(((bf16[32,6,1792]{2,1,0:T(8,128)(2,1)}), bf16[32,6,1792]{2,1,0:T(8,128)(2,1)S(1)}, u32[]{:S(2)}, u32[]{:S(2)}) %all-to-all-start) | async-done | bytes 688160 | tf_op jit(solution)/shard_map/all_to_all | solution.py:75
  47.0 0.2 reshape.255
  47.2 0.9 gather_fusion.1
  48.2 0.2 convert_reduce_fusion
  48.4 0.3 fusion.31
  48.7 32.5 %all-gather.3.cloned.1.call-done = bf16[1792,2688]{1,0:T(8,128)(2,1)} async-done(((bf16[112,2688]{1,0:T(8,128)(2,1)}), bf16[1792,2688]{1,0:T(8,128)(2,1)}) %all-gather.3.cloned.1.call-update) | async-done | bytes 9633808 | tf_op jit(solution)/shard_map/all_gather | solution.py:81
  81.3 5.4 %convolution_convert_fusion = bf16[128,2688]{1,0:T(8,128)(2,1)S(1)} fusion(bf16[1792,2688]{1,0:T(8,128)(2,1)} %all-gather.3.cloned.1.call-done, f32[1792]{0:T(1024)S(1)} %copy-done.10, f32[128]{0:T(128)S(1)} %add_rsqrt_fusion, f32[128]{0:T(128)S(1)} %broadcast_multiply_fusion.2, bf16[128,1792]{1,0:T(8,128)(2,1)S(1)} %gather_fusion.1, ...), kind=kOutput, calls=%fused_computation.6 | convolution fusion | flops 1234845696 | bytes 10788992 | tf_op jit(solution)/shard_map/dot_general | solution.py:85
  86.7 0.9 fusion.97
  87.6 1.9 collective-permute-start
  89.5 2.4 %collective-permute-start.1 = (bf16[96,1792]{1,0:T(8,128)(2,1)}, bf16[96,1792]{1,0:T(8,128)(2,1)}, u32[]{:S(2)}, u32[]{:S(2)}) collective-permute-start(bf16[96,1792]{1,0:T(8,128)(2,1)} %get-tuple-element.33), channel_id=1, source_target_pairs={{1,0},{2,1},{3,2},{4,3},{5,4},{6,5},{7,6},{8,7},{9,8},{10,9},{11,1... | collective-permute-start | bytes 1032200 | tf_op jit(solution)/shard_map/ppermute | solution.py:19
  91.9 0.1 broadcast_compare_fusion
  92.1 34.0 %all-gather.5.cloned.1.call-done = bf16[896,1792]{1,0:T(8,128)(2,1)} async-done(((bf16[56,1792]{1,0:T(8,128)(2,1)}), bf16[896,1792]{1,0:T(8,128)(2,1)}) %all-gather.5.cloned.1.call-update) | async-done | bytes 3211280 | tf_op jit(solution)/shard_map/all_gather | solution.py:82
  126.0 3.0 %convolution_convert_fusion.1 = bf16[128,896]{1,0:T(8,128)(2,1)S(1)} fusion(bf16[896,1792]{1,0:T(8,128)(2,1)} %all-gather.5.cloned.1.call-done, bf16[1,128,1792]{2,1,0:T(8,128)(2,1)S(1)} %copy-done.4), kind=kOutput, calls=%fused_computation.28 | convolution fusion | flops 411156480 | bytes 3899392 | tf_op jit(solution)/shard_map/dot_general | solution.py:98
  129.1 0.2 copy.25
  129.3 0.8 copy.22
  130.2 1.1 pad_maximum_fusion
  131.2 0.1 fusion.96
  131.3 1.6 reshape.258
  132.9 0.8 reshape.256
  133.7 0.3 fusion.41
  134.0 3.2 %fusion.98 = (f32[8,128]{1,0:T(8,128)S(1)}, f32[8,128,320]{1,2,0:T(8,128)}) fusion(pred[128,320]{0,1:T(8,128)(4,1)S(1)} %broadcast_compare_fusion, bf16[128,8,112]{0,2,1:T(8,128)(2,1)} %bitcast.59, bf16[320,8,112]{2,1,0:T(8,128)(2,1)} %reshape.258), kind=kOutput, calls=%fused_computation.111 | convolution fusion | flops 74711360 | bytes 2158592 | tf_op jit(solution)/shard_map/sub | solution.py:49
  137.3 3.0 %convolution_bitcast_fusion = f32[320,8,112]{2,0,1:T(8,128)} fusion(bf16[128,8,112]{0,2,1:T(8,128)(2,1)S(1)} %bitcast.58, f32[8,128]{1,0:T(8,128)S(1)} %get-tuple-element.40, pred[128,320]{0,1:T(8,128)(4,1)S(1)} %broadcast_compare_fusion, bf16[128,8,112]{0,2,1:T(8,128)(2,1)} %bitcast.60, bf16[320,8,112]{2,1,0:T(8,128)(2,1)} %reshape.258), kind=kOutput, calls=%fused_computation.17 | convolution fusion | flops 148440384 | bytes 2224128 | tf_op jit(solution)/shard_map/hqk,qhd->khd/dot_general | solution.py:113
  140.3 3.4 %convolution_bitcast_fusion.1 = f32[320,8,112]{2,0,1:T(8,128)} fusion(bf16[128,8,112]{0,2,1:T(8,128)(2,1)S(1)} %bitcast.61, f32[8,128,320]{1,2,0:T(8,128)S(1)} %fusion.41, f32[8,128,320]{1,2,0:T(8,128)} %get-tuple-element.41, f32[8,128]{1,0:T(8,128)S(1)} %get-tuple-element.40), kind=kOutput, calls=%fused_computation.18 | convolution fusion | flops 75695424 | bytes 4001792 | tf_op jit(solution)/shard_map/hqk,qhd->khd/dot_general | solution.py:112
  143.7 2.1 copy.28
  145.8 1.4 reshape.262
  147.2 2.1 copy.29
  149.3 1.4 reshape.263
  150.7 1.4 constant_dynamic-update-slice_fusion.1
  152.1 0.2 copy-done.1
  152.3 0.1 constant_dynamic-update-slice_fusion
  152.4 1.2 fusion.95
  153.6 3.4 %collective-permute-start.4 = (f32[96,1792]{1,0:T(8,128)}, f32[96,1792]{1,0:T(8,128)}, u32[]{:S(2)}, u32[]{:S(2)}) collective-permute-start(f32[96,1792]{1,0:T(8,128)} %get-tuple-element.29), channel_id=1, source_target_pairs={{0,1},{1,2},{2,3},{3,4},{4,5},{5,6},{6,7},{7,8},{8,9},{9,10},{10,1... | collective-permute-start | bytes 2064392 | tf_op jit(solution)/shard_map/ppermute | solution.py:16
  157.0 1.0 slice.111
  158.0 1.9 collective-permute-start.5
  159.9 4.3 %fusion.17 = bf16[8,112,128]{2,1,0:T(8,128)(2,1)} fusion(f32[8,128,320]{1,2,0:T(8,128)} %copy-done.6, bf16[320,8,112]{2,1,0:T(8,128)(2,1)} %reshape.258, f32[8,128,320]{1,2,0:T(8,128)} %get-tuple-element.41, f32[8,128]{1,0:T(8,128)S(1)} %get-tuple-element.40), kind=kOutput, calls=%fused_computation.27 | convolution fusion | flops 75810112 | bytes 3428352 | tf_op jit(solution)/shard_map/hqk,khd->qhd/dot_general | solution.py:108
  164.3 1.8 copy.30
  166.0 2.0 fusion.33
  168.1 2.5 %collective-permute-done.5 = f32[96,1792]{1,0:T(8,128)} collective-permute-done((f32[96,1792]{1,0:T(8,128)}, f32[96,1792]{1,0:T(8,128)}, u32[]{:S(2)}, u32[]{:S(2)}) %collective-permute-start.5) | collective-permute-done | bytes 688160 | tf_op jit(solution)/shard_map/ppermute | solution.py:19
  170.6 2.3 fusion.32
  172.8 1.2 convert.9
  174.1 6.6 %fusion.94 = (f32[128]{0:T(128)S(1)}, f32[128]{0:T(128)S(1)}, f32[128,1792]{1,0:T(8,128)S(1)}) fusion(f32[128]{0:T(128)S(1)} %add_rsqrt_fusion, f32[128]{0:T(128)S(1)} %broadcast_multiply_fusion.2, bf16[128,1792]{1,0:T(8,128)(2,1)S(1)} %gather_fusion.1, pred[128]{0:T(512)(128)(4,1)S(1)} %compare_and_fusion.1, f32[1792]{0:T(1024)S(1)} %copy-done.10, ...), kind=kOutput, calls=%fused_computation.107 | convolution fusion | flops 1236336384 | bytes 11707520 | tf_op jit(solution)/shard_map/dot_general | solution.py:126
  180.7 1.9 scatter_custom_fusion
  182.6 1.2 reshape.264
  183.8 9.4 %all-to-all-start.1 = ((bf16[32,6,1792]{2,1,0:T(8,128)(2,1)}), bf16[32,6,1792]{2,1,0:T(8,128)(2,1)S(1)}, u32[]{:S(2)}, u32[]{:S(2)}) async-start(bf16[32,6,1792]{2,1,0:T(8,128)(2,1)} %reshape.264), calls=%async_computation.1 | async-start | bytes 1835008 | tf_op jit(solution)/shard_map/all_to_all | solution.py:140
  193.2 2.0 convolution_convert_fusion.2
  195.2 3.3 %fusion.3 = bf16[1,128,1792]{2,1,0:T(8,128)(2,1)} fusion(bf16[128,896]{0,1:T(8,128)(2,1)S(1)} %bitcast.64, bf16[896,1792]{1,0:T(8,128)(2,1)} %all-gather.5.cloned.1.call-done, bf16[128,1792]{1,0:T(8,128)(2,1)S(1)} %gather_fusion.1, pred[128]{0:T(512)(128)(4,1)S(1)} %compare_and_fusion.1), kind=kOutput, calls=%fused_computation.10 | convolution fusion | flops 411959296 | bytes 4358272 | tf_op jit(solution)/shard_map/dot_general | solution.py:94
  198.5 17.8 %all-to-all-done.1 = bf16[32,6,1792]{2,1,0:T(8,128)(2,1)S(1)} async-done(((bf16[32,6,1792]{2,1,0:T(8,128)(2,1)}), bf16[32,6,1792]{2,1,0:T(8,128)(2,1)S(1)}, u32[]{:S(2)}, u32[]{:S(2)}) %all-to-all-start.1) | async-done | bytes 688160 | tf_op jit(solution)/shard_map/all_to_all | solution.py:140
  216.3 0.2 reshape.294
  216.5 3.1 %scatter_custom_fusion.1 = bf16[193,1792]{1,0:T(8,128)(2,1)S(1)} fusion(s32[192]{0:T(256)S(1)} %bitcast.66, bf16[192,1792]{1,0:T(8,128)(2,1)S(1)} %reshape.294, bf16[]{:T(256)} %constant.97.clone.1), kind=kCustom, calls=%fused_computation.73 | custom fusion | flops 344064 | bytes 691714 | tf_op jit(solution)/shard_map/scatter-add | solution.py:144
  219.6 0.9 slice_bitcast_fusion
  (43 shorter events, 0.3 us)
Async XLA Ops:
  7.2 3.2 %copy-start = (bf16[1,192,1792]{2,1,0:T(8,128)(2,1)S(1)}, bf16[1,192,1792]{2,1,0:T(8,128)(2,1)}, u32[]{:S(2)}) copy-start(bf16[1,192,1792]{2,1,0:T(8,128)(2,1)} %param.12) | copy-start | bytes 2064388
  7.2 74.1 %all-gather.3.cloned.1.call-start = ((), (), s32[]{:S(2)}) async-start(), calls=%async_computation.2 | async-start | bytes 10235904 | tf_op jit(solution)/shard_map/all_gather | solution.py:81
  7.9 118.1 %all-gather.5.cloned.1.call-start = ((), (), s32[]{:S(2)}) async-start(), calls=%async_computation.3 | async-start | bytes 3411968 | tf_op jit(solution)/shard_map/all_gather | solution.py:82
  12.9 10.6 %copy-start.11 = (s32[1,128]{1,0:T(1,128)S(1)}, s32[1,128]{1,0:T(1,128)}, u32[]{:S(2)}) copy-start(s32[1,128]{1,0:T(1,128)} %param.15) | copy-start | bytes 1540
  12.9 17.5 %copy-start.12 = (s32[1,128]{1,0:T(1,128)S(1)}, s32[1,128]{1,0:T(1,128)}, u32[]{:S(2)}) copy-start(s32[1,128]{1,0:T(1,128)} %param.14) | copy-start | bytes 1540
  12.9 34.1 %all-to-all-start = ((bf16[32,6,1792]{2,1,0:T(8,128)(2,1)}), bf16[32,6,1792]{2,1,0:T(8,128)(2,1)S(1)}, u32[]{:S(2)}, u32[]{:S(2)}) async-start(bf16[32,6,1792]{2,1,0:T(8,128)(2,1)} %broadcast_select_fusion), calls=%async_computation | async-start | bytes 1835008 | tf_op jit(solution)/shard_map/all_to_all | solution.py:75
  23.6 6.8 %collective-permute-start.2 = (s32[96]{0:T(128)S(1)}, s32[96]{0:T(128)S(1)}, u32[]{:S(2)}, u32[]{:S(2)}) collective-permute-start(s32[96]{0:T(128)S(1)} %get-tuple-element.36), channel_id=1, source_target_pairs={{0,1},{1,2},{2,3},{3,4},{4,5},{5,6},{6,7},{7,8},{8,9},{9,10},{10,1... | collective-permute-start | bytes 1160 | tf_op jit(solution)/shard_map/ppermute | solution.py:16
  28.5 5.3 %collective-permute-start.3 = (s32[96]{0:T(128)S(1)}, s32[96]{0:T(128)S(1)}, u32[]{:S(2)}, u32[]{:S(2)}) collective-permute-start(s32[96]{0:T(128)S(1)} %get-tuple-element.37), channel_id=1, source_target_pairs={{1,0},{2,1},{3,2},{4,3},{5,4},{6,5},{7,6},{8,7},{9,8},{10,9},{11,1... | collective-permute-start | bytes 1160 | tf_op jit(solution)/shard_map/ppermute | solution.py:19
  47.2 34.1 %copy-start.10 = (f32[1792]{0:T(1024)S(1)}, f32[1792]{0:T(1024)}, u32[]{:S(2)}) copy-start(f32[1792]{0:T(1024)} %param.16) | copy-start | bytes 21508
  86.7 39.3 %copy-start.4 = (bf16[1,128,1792]{2,1,0:T(8,128)(2,1)S(1)}, bf16[1,128,1792]{2,1,0:T(8,128)(2,1)}, u32[]{:S(2)}) copy-start(bf16[1,128,1792]{2,1,0:T(8,128)(2,1)} %param.19) | copy-start | bytes 1376260
  87.6 42.6 %collective-permute-start = (bf16[96,1792]{1,0:T(8,128)(2,1)}, bf16[96,1792]{1,0:T(8,128)(2,1)S(1)}, u32[]{:S(2)}, u32[]{:S(2)}) collective-permute-start(bf16[96,1792]{1,0:T(8,128)(2,1)} %get-tuple-element.32), channel_id=1, source_target_pairs={{0,1},{1,2},{2,3},{3,4},{4,5},{5,6},{6,7},{7,8},{8,9},{9,10},{10,1... | collective-permute-start | bytes 1032200 | tf_op jit(solution)/shard_map/ppermute | solution.py:16
  89.5 40.6 %collective-permute-start.1 = (bf16[96,1792]{1,0:T(8,128)(2,1)}, bf16[96,1792]{1,0:T(8,128)(2,1)}, u32[]{:S(2)}, u32[]{:S(2)}) collective-permute-start(bf16[96,1792]{1,0:T(8,128)(2,1)} %get-tuple-element.33), channel_id=1, source_target_pairs={{1,0},{2,1},{3,2},{4,3},{5,4},{6,5},{7,6},{8,7},{9,8},{10,9},{11,1... | collective-permute-start | bytes 1032200 | tf_op jit(solution)/shard_map/ppermute | solution.py:19
  133.7 3.6 %copy-start.2 = (bf16[320,8,112]{2,1,0:T(8,128)(2,1)}, bf16[320,8,112]{2,1,0:T(8,128)(2,1)S(1)}, u32[]{:S(2)}) copy-start(bf16[320,8,112]{2,1,0:T(8,128)(2,1)S(1)} %reshape.256) | copy-start | bytes 1720324
  134.0 6.3 %copy-start.6 = (f32[8,128,320]{1,2,0:T(8,128)}, f32[8,128,320]{1,2,0:T(8,128)S(1)}, u32[]{:S(2)}) copy-start(f32[8,128,320]{1,2,0:T(8,128)S(1)} %fusion.41) | copy-start | bytes 3932164
  137.3 3.0 %copy-start.7 = (bf16[128,896]{0,1:T(8,128)(2,1)S(1)}, bf16[128,896]{0,1:T(8,128)(2,1)}, u32[]{:S(2)}) copy-start(bf16[128,896]{0,1:T(8,128)(2,1)} %copy.22) | copy-start | bytes 688132
  150.7 1.6 copy-start.1
  153.6 12.5 %collective-permute-start.4 = (f32[96,1792]{1,0:T(8,128)}, f32[96,1792]{1,0:T(8,128)}, u32[]{:S(2)}, u32[]{:S(2)}) collective-permute-start(f32[96,1792]{1,0:T(8,128)} %get-tuple-element.29), channel_id=1, source_target_pairs={{0,1},{1,2},{2,3},{3,4},{4,5},{5,6},{6,7},{7,8},{8,9},{9,10},{10,1... | collective-permute-start | bytes 2064392 | tf_op jit(solution)/shard_map/ppermute | solution.py:16
  158.0 12.6 %collective-permute-start.5 = (f32[96,1792]{1,0:T(8,128)}, f32[96,1792]{1,0:T(8,128)}, u32[]{:S(2)}, u32[]{:S(2)}) collective-permute-start(f32[96,1792]{1,0:T(8,128)} %get-tuple-element.28), channel_id=1, source_target_pairs={{1,0},{2,1},{3,2},{4,3},{5,4},{6,5},{7,6},{8,7},{9,8},{10,9},{11,1... | collective-permute-start | bytes 2064392 | tf_op jit(solution)/shard_map/ppermute | solution.py:19
  168.1 6.0 %copy-start.9 = (bf16[128,896]{1,0:T(8,128)(2,1)S(1)}, bf16[128,896]{1,0:T(8,128)(2,1)}, u32[]{:S(2)}) copy-start(bf16[128,896]{1,0:T(8,128)(2,1)} %copy.30) | copy-start | bytes 688132
  174.1 6.7 %copy-start.5 = (bf16[1,128,1792]{2,1,0:T(8,128)(2,1)S(1)}, bf16[1,128,1792]{2,1,0:T(8,128)(2,1)}, u32[]{:S(2)}) copy-start(bf16[1,128,1792]{2,1,0:T(8,128)(2,1)} %param.19) | copy-start | bytes 1376260
  183.8 9.4 %copy-start.3 = (bf16[320,8,112]{2,1,0:T(8,128)(2,1)S(1)}, bf16[320,8,112]{2,1,0:T(8,128)(2,1)}, u32[]{:S(2)}) copy-start(bf16[320,8,112]{2,1,0:T(8,128)(2,1)} %copy-done.2) | copy-start | bytes 1720324
  183.8 9.4 %copy-start.8 = (bf16[128,896]{0,1:T(8,128)(2,1)S(1)}, bf16[128,896]{0,1:T(8,128)(2,1)}, u32[]{:S(2)}) copy-start(bf16[128,896]{0,1:T(8,128)(2,1)} %copy.22) | copy-start | bytes 688132
  183.8 32.5 %all-to-all-start.1 = ((bf16[32,6,1792]{2,1,0:T(8,128)(2,1)}), bf16[32,6,1792]{2,1,0:T(8,128)(2,1)S(1)}, u32[]{:S(2)}, u32[]{:S(2)}) async-start(bf16[32,6,1792]{2,1,0:T(8,128)(2,1)} %reshape.264), calls=%async_computation.1 | async-start | bytes 1835008 | tf_op jit(solution)/shard_map/all_to_all | solution.py:140
Sparse Core Ops, SparseCore 0:
  10.1 71.1 all-gather.2
  83.4 42.5 all-gather.4
where the time goes:
time: 228 us; the launch traced here: 227 us
  waiting for transfers between devices  105 us (46%)
  starting transfers between devices  36.5 us (16%)
  matrix products  34.7 us (15%)
  local copies, waits for them, and re-layouts  23 us (10%)
  between operations  14.4 us (6%)
  other arithmetic  14.2 us (6%)
    all_gather x1, waiting for transfers between devices, local(): lax.all_gather(out_weight, 'tensor', axis=0, tiled=True)  34 us
    all_gather x1, waiting for transfers between devices, local(): lax.all_gather(qkv_weight, 'tensor', axis=0, tiled=True)  32.5 us
    all_to_all x1, waiting for transfers between devices, local(): lax.all_to_all(back_slots, 'dp', split_axis=0, concat_axis=0, tiled=True)  17.8 us
    all_to_all x1, waiting for transfers between devices, local(): lax.all_to_all(outgoing, 'dp', split_axis=0, concat_axis=0, tiled=True)  13.2 us
    all_to_all x1, starting transfers between devices, local(): lax.all_to_all(outgoing, 'dp', split_axis=0, concat_axis=0, tiled=True)  10.6 us
    ppermute x3, starting transfers between devices, extended(): lax.ppermute(lax.slice_in_dim(block, block.shape[dim] - width, None, axis...  10.1 us
    all_to_all x1, starting transfers between devices, local(): lax.all_to_all(back_slots, 'dp', split_axis=0, concat_axis=0, tiled=True)  9.4 us
    dot_general x1, matrix products, local(): lax.dot_general(grad_proj, full_qkv, (((1,), (1,)), ((), ())), preferred_...  6.63 us
  transfers between devices with their start and end apart: 10, of which 6 were waited for; matrix products, arithmetic and copies ran while one was open for 14% of the time, Pallas kernels for 0%

commit v1 on v0

--- a/solution.py
+++ b/solution.py
@@ -77,8 +77,11 @@
     )
     pick_rows = take_rows[0]
     packed = jnp.take(incoming, pick_rows, axis=0)
+    divide_patches = lambda local_array: jnp.concatenate(
+        lax.all_to_all(jnp.stack([local_array] * lax.psum(1, "tensor")), "tensor", 0, 0), axis=0
+    )
     full_qkv, full_out = (
-        lax.all_gather(qkv_weight, "tensor", axis=0, tiled=True),
+        divide_patches(qkv_weight),
         lax.all_gather(out_weight, "tensor", axis=0, tiled=True),
     )
     values, unit_rows, inv_dev, normed = normalize(packed, norm_gain)

time: 228 us -> 403 us (1.77)
  waiting for transfers between devices: 105 us -> 239 us
  blocking collectives: 0 us -> 33.9 us
  local copies, waits for them, and re-layouts: 23 us -> 29.7 us
    ppermute x3, waiting for transfers between devices: 5.77 us -> 221 us  [extended(): lax.ppermute(lax.slice_in_dim(block, 0, width, axis=dim), axis, backward)]
    all_gather x1, waiting for transfers between devices: 34 us -> 0.02 us  [local(): lax.all_gather(out_weight, 'tensor', axis=0, tiled=True)]
    all_to_all x0 -> x1, blocking collectives: none -> 33.9 us  [local(): lax.all_to_all(outgoing, 'dp', split_axis=0, concat_axis=0, tiled=True)]
    all_gather x1 -> x0, waiting for transfers between devices: 32.5 us -> none  [local(): lax.all_gather(qkv_weight, 'tensor', axis=0, tiled=True)]
    all_to_all x1, waiting for transfers between devices: 13.2 us -> 0.01 us  [local(): lax.all_to_all(jnp.stack([local_array] * lax.psum(1, 'tensor')), 'tensor'...]
    another operation x0 -> x1, local copies, waits for them, and re-layouts: none -> 4.35 us  [local(): jnp.stack([local_array] * lax.psum(1, 'tensor'))]
    all_to_all x1, starting transfers between devices: 9.4 us -> 5.31 us  [local(): lax.all_to_all(back_slots, 'dp', split_axis=0, concat_axis=0, tiled=True)]
  transfers between devices with their start and end apart: 10 -> 9, of which waited for: 6 -> 3; matrix products, arithmetic and copies ran while one was open for 14% -> 7% of each run, Pallas kernels for 0% -> 0%
where the time goes in v1:
time: 403 us; the launch traced here: 401 us
  waiting for transfers between devices  239 us (59%)
  starting transfers between devices  36.5 us (9%)
  matrix products  34.4 us (9%)
  blocking collectives  33.9 us (8%)
  local copies, waits for them, and re-layouts  29.7 us (7%)
  between operations  14.5 us (4%)
  other arithmetic  13.2 us (3%)
    ppermute x3, waiting for transfers between devices, extended(): lax.ppermute(lax.slice_in_dim(block, 0, width, axis=dim), axis, backward)  221 us
    all_to_all x1, blocking collectives, local(): lax.all_to_all(outgoing, 'dp', split_axis=0, concat_axis=0, tiled=True)  33.9 us
    all_to_all x1, waiting for transfers between devices, local(): lax.all_to_all(back_slots, 'dp', split_axis=0, concat_axis=0, tiled=True)  17.2 us
    all_to_all x1, starting transfers between devices, local(): lax.all_to_all(jnp.stack([local_array] * lax.psum(1, 'tensor')), 'tensor'...  13.6 us
    ppermute x3, starting transfers between devices, extended(): lax.ppermute(lax.slice_in_dim(block, block.shape[dim] - width, None, axis...  11.7 us
  transfers between devices with their start and end apart: 9, of which 3 were waited for; matrix products, arithmetic and copies ran while one was open for 7% of the time, Pallas kernels for 0%

profile of v1, /device:TPU:1, one launch (start us, length us, event | category | flops | bytes accessed | tf_op | source)
XLA Modules:
  0.0 400.8 jit_solution(2146544869960887471)
XLA Ops:
  7.2 0.8 copy.21
  8.0 0.7 compare_and_fusion
  8.7 0.1 reshape.259
  8.8 1.1 gather_fusion
  10.0 0.2 gather.11
  10.2 0.1 copy.20
  10.3 0.1 broadcast_select_fusion
  10.5 33.9 %all_to_all.15 = bf16[32,6,1792]{2,1,0:T(8,128)(2,1)S(1)} all-to-all(bf16[32,6,1792]{2,1,0:T(8,128)(2,1)S(1)} %broadcast_select_fusion), channel_id=1, replica_groups=mesh['dp'=32,'tensor'=16] {'dp'}, dimensions={0} | all-to-all | bytes 1376256 | tf_op jit(solution)/shard_map/all_to_all | solution.py:75
  44.4 4.3 %stack.2 = bf16[16,112,2688]{2,1,0:T(8,128)(2,1)} broadcast(bf16[112,2688]{1,0:T(8,128)(2,1)S(1)} %copy-done.7), dimensions={1,2} | broadcast | bytes 10235904 | tf_op jit(solution)/shard_map/stack | solution.py:81
  48.7 13.6 %all-to-all-start.1 = ((bf16[16,112,2688]{2,1,0:T(8,128)(2,1)}), bf16[16,112,2688]{2,1,0:T(8,128)(2,1)}, u32[]{:S(2)}, u32[]{:S(2)}) async-start(bf16[16,112,2688]{2,1,0:T(8,128)(2,1)} %stack.2), calls=%async_computation.1 | async-start | bytes 19267584 | tf_op jit(solution)/shard_map/all_to_all | solution.py:81
  62.3 0.0 all-gather.2.cloned.1.call-start
  62.3 0.7 all-gather.2.cloned.1.call-update
  63.0 0.1 slice_bitcast_fusion.2
  63.1 2.0 collective-permute-start.3
  65.2 3.5 collective-permute-start.2
  68.7 218.1 %collective-permute-done.3 = s32[96]{0:T(128)S(1)} collective-permute-done((s32[96]{0:T(128)S(1)}, s32[96]{0:T(128)S(1)}, u32[]{:S(2)}, u32[]{:S(2)}) %collective-permute-start.3) | collective-permute-done | bytes 416 | tf_op jit(solution)/shard_map/ppermute | solution.py:19
  286.8 0.1 pad_add_fusion
  286.9 0.2 reshape.260
  287.1 0.9 gather_fusion.1
  288.1 0.2 convert_reduce_fusion
  288.3 0.3 fusion.31
  288.7 5.4 %convolution_convert_fusion = bf16[128,2688]{1,0:T(8,128)(2,1)S(1)} fusion(bf16[1792,2688]{1,0:T(8,128)(2,1)} %bitcast.5, f32[1792]{0:T(1024)S(1)} %copy-done.11, f32[128]{0:T(128)S(1)} %add_rsqrt_fusion, f32[128]{0:T(128)S(1)} %broadcast_multiply_fusion.2, bf16[128,1792]{1,0:T(8,128)(2,1)S(1)} %gather_fusion.1, pred[128]{0:T(512)(128)(4,1)S(1)} %compare_and_fusion.1), kind=kOutput, calls=%fused_computation.6 | convolution fusion | flops 1234845696 | bytes 10788992 | tf_op jit(solution)/shard_map/dot_general | solution.py:88
  294.1 0.9 fusion.97
  295.0 1.9 collective-permute-start.1
  296.9 3.8 collective-permute-start
  300.7 0.1 broadcast_compare_fusion
  300.9 3.0 convolution_convert_fusion.1
  303.9 0.2 copy.25
  304.1 0.9 copy.22
  305.0 1.1 pad_maximum_fusion
  306.1 0.1 fusion.96
  306.2 0.8 reshape.262
  306.9 1.6 reshape.264
  308.6 0.3 fusion.41
  308.9 3.2 fusion.98
  312.1 3.0 convolution_bitcast_fusion
  315.1 3.4 convolution_bitcast_fusion.1
  318.5 2.1 copy.28
  320.6 1.4 reshape.268
  322.0 1.4 constant_dynamic-update-slice_fusion.1
  323.4 0.2 copy-done.5
  323.6 1.9 copy.29
  325.5 2.6 reshape.269
  328.1 1.3 constant_dynamic-update-slice_fusion
  329.5 1.2 fusion.95
  330.7 4.4 %collective-permute-start.4 = (f32[96,1792]{1,0:T(8,128)}, f32[96,1792]{1,0:T(8,128)}, u32[]{:S(2)}, u32[]{:S(2)}) collective-permute-start(f32[96,1792]{1,0:T(8,128)} %get-tuple-element.29), channel_id=1, source_target_pairs={{0,1},{1,2},{2,3},{3,4},{4,5},{5,6},{6,7},{7,8},{8,9},{9,10},{10,1... | collective-permute-start | bytes 2064392 | tf_op jit(solution)/shard_map/ppermute | solution.py:16
  335.1 1.0 slice.111
  336.1 1.9 collective-permute-start.5
  338.0 4.2 %fusion.17 = bf16[8,112,128]{2,1,0:T(8,128)(2,1)} fusion(f32[8,128,320]{1,2,0:T(8,128)} %copy-done.6, bf16[320,8,112]{2,1,0:T(8,128)(2,1)} %reshape.264, f32[8,128,320]{1,2,0:T(8,128)} %get-tuple-element.41, f32[8,128]{1,0:T(8,128)S(1)} %get-tuple-element.40), kind=kOutput, calls=%fused_computation.27 | convolution fusion | flops 75810112 | bytes 3428352 | tf_op jit(solution)/shard_map/hqk,khd->qhd/dot_general | solution.py:111
  342.2 1.8 copy.30
  344.0 2.0 fusion.33
  346.0 2.7 collective-permute-done.5
  348.7 2.3 fusion.32
  350.9 1.2 convert.9
  352.2 6.6 %fusion.94 = (f32[128]{0:T(128)S(1)}, f32[128]{0:T(128)S(1)}, f32[128,1792]{1,0:T(8,128)S(1)}) fusion(f32[128]{0:T(128)S(1)} %add_rsqrt_fusion, f32[128]{0:T(128)S(1)} %broadcast_multiply_fusion.2, bf16[128,1792]{1,0:T(8,128)(2,1)S(1)} %gather_fusion.1, pred[128]{0:T(512)(128)(4,1)S(1)} %compare_and_fusion.1, f32[1792]{0:T(1024)S(1)} %copy-done.11, ...), kind=kOutput, calls=%fused_computation.107 | convolution fusion | flops 1236336384 | bytes 11707520 | tf_op jit(solution)/shard_map/dot_general | solution.py:129
  358.8 1.9 scatter_custom_fusion
  360.7 1.1 reshape.270
  361.9 5.3 %all-to-all-start.2 = ((bf16[32,6,1792]{2,1,0:T(8,128)(2,1)}), bf16[32,6,1792]{2,1,0:T(8,128)(2,1)S(1)}, u32[]{:S(2)}, u32[]{:S(2)}) async-start(bf16[32,6,1792]{2,1,0:T(8,128)(2,1)} %reshape.270), calls=%async_computation.2 | async-start | bytes 1835008 | tf_op jit(solution)/shard_map/all_to_all | solution.py:143
  367.2 2.0 convolution_convert_fusion.2
  369.2 3.4 fusion.3
  372.5 17.2 %all-to-all-done.2 = bf16[32,6,1792]{2,1,0:T(8,128)(2,1)S(1)} async-done(((bf16[32,6,1792]{2,1,0:T(8,128)(2,1)}), bf16[32,6,1792]{2,1,0:T(8,128)(2,1)S(1)}, u32[]{:S(2)}, u32[]{:S(2)}) %all-to-all-start.2) | async-done | bytes 688160 | tf_op jit(solution)/shard_map/all_to_all | solution.py:143
  389.7 0.2 reshape.300
  389.9 3.1 scatter_custom_fusion.1
  393.1 0.9 slice_bitcast_fusion
  (44 shorter events, 0.2 us)
Async XLA Ops:
  7.2 1.7 copy-start
  10.5 33.9 %copy-start.7 = (bf16[112,2688]{1,0:T(8,128)(2,1)S(1)}, bf16[112,2688]{1,0:T(8,128)(2,1)}, u32[]{:S(2)}) copy-start(bf16[112,2688]{1,0:T(8,128)(2,1)} %param.17) | copy-start | bytes 1806340
  48.7 14.3 %copy-start.12 = (s32[1,128]{1,0:T(1,128)S(1)}, s32[1,128]{1,0:T(1,128)}, u32[]{:S(2)}) copy-start(s32[1,128]{1,0:T(1,128)} %param.15) | copy-start | bytes 1540
  48.7 20.0 %copy-start.13 = (s32[1,128]{1,0:T(1,128)S(1)}, s32[1,128]{1,0:T(1,128)}, u32[]{:S(2)}) copy-start(s32[1,128]{1,0:T(1,128)} %param.14) | copy-start | bytes 1540
  48.7 239.9 %all-to-all-start.1 = ((bf16[16,112,2688]{2,1,0:T(8,128)(2,1)}), bf16[16,112,2688]{2,1,0:T(8,128)(2,1)}, u32[]{:S(2)}, u32[]{:S(2)}) async-start(bf16[16,112,2688]{2,1,0:T(8,128)(2,1)} %stack.2), calls=%async_computation.1 | async-start | bytes 19267584 | tf_op jit(solution)/shard_map/all_to_all | solution.py:81
  62.3 238.6 %all-gather.2.cloned.1.call-start = ((), (), s32[]{:S(2)}) async-start(), calls=%async_computation.3 | async-start | bytes 3411968 | tf_op jit(solution)/shard_map/all_gather | solution.py:85
  63.1 223.7 %collective-permute-start.3 = (s32[96]{0:T(128)S(1)}, s32[96]{0:T(128)S(1)}, u32[]{:S(2)}, u32[]{:S(2)}) collective-permute-start(s32[96]{0:T(128)S(1)} %get-tuple-element.37), channel_id=1, source_target_pairs={{1,0},{2,1},{3,2},{4,3},{5,4},{6,5},{7,6},{8,7},{9,8},{10,9},{11,1... | collective-permute-start | bytes 1160 | tf_op jit(solution)/shard_map/ppermute | solution.py:19
  65.2 221.7 %collective-permute-start.2 = (s32[96]{0:T(128)S(1)}, s32[96]{0:T(128)S(1)}, u32[]{:S(2)}, u32[]{:S(2)}) collective-permute-start(s32[96]{0:T(128)S(1)} %get-tuple-element.36), channel_id=1, source_target_pairs={{0,1},{1,2},{2,3},{3,4},{4,5},{5,6},{6,7},{7,8},{8,9},{9,10},{10,1... | collective-permute-start | bytes 1160 | tf_op jit(solution)/shard_map/ppermute | solution.py:16
  287.1 1.5 copy-start.11
  294.1 6.8 %copy-start.3 = (bf16[1,128,1792]{2,1,0:T(8,128)(2,1)S(1)}, bf16[1,128,1792]{2,1,0:T(8,128)(2,1)}, u32[]{:S(2)}) copy-start(bf16[1,128,1792]{2,1,0:T(8,128)(2,1)} %param.19) | copy-start | bytes 1376260
  295.0 10.0 %collective-permute-start.1 = (bf16[96,1792]{1,0:T(8,128)(2,1)}, bf16[96,1792]{1,0:T(8,128)(2,1)S(1)}, u32[]{:S(2)}, u32[]{:S(2)}) collective-permute-start(bf16[96,1792]{1,0:T(8,128)(2,1)} %get-tuple-element.33), channel_id=1, source_target_pairs={{1,0},{2,1},{3,2},{4,3},{5,4},{6,5},{7,6},{8,7},{9,8},{10,9},{11,1... | collective-permute-start | bytes 1032200 | tf_op jit(solution)/shard_map/ppermute | solution.py:19
  296.9 8.1 %collective-permute-start = (bf16[96,1792]{1,0:T(8,128)(2,1)}, bf16[96,1792]{1,0:T(8,128)(2,1)}, u32[]{:S(2)}, u32[]{:S(2)}) collective-permute-start(bf16[96,1792]{1,0:T(8,128)(2,1)} %get-tuple-element.32), channel_id=1, source_target_pairs={{0,1},{1,2},{2,3},{3,4},{4,5},{5,6},{6,7},{7,8},{8,9},{9,10},{10,1... | collective-permute-start | bytes 1032200 | tf_op jit(solution)/shard_map/ppermute | solution.py:16
  306.9 1.9 copy-start.1
  308.9 6.2 %copy-start.6 = (f32[8,128,320]{1,2,0:T(8,128)}, f32[8,128,320]{1,2,0:T(8,128)S(1)}, u32[]{:S(2)}) copy-start(f32[8,128,320]{1,2,0:T(8,128)S(1)} %fusion.41) | copy-start | bytes 3932164
  308.9 3.2 copy-start.8
  322.0 1.7 copy-start.5
  330.7 13.3 %collective-permute-start.4 = (f32[96,1792]{1,0:T(8,128)}, f32[96,1792]{1,0:T(8,128)}, u32[]{:S(2)}, u32[]{:S(2)}) collective-permute-start(f32[96,1792]{1,0:T(8,128)} %get-tuple-element.29), channel_id=1, source_target_pairs={{0,1},{1,2},{2,3},{3,4},{4,5},{5,6},{6,7},{7,8},{8,9},{9,10},{10,1... | collective-permute-start | bytes 2064392 | tf_op jit(solution)/shard_map/ppermute | solution.py:16
  336.1 12.6 %collective-permute-start.5 = (f32[96,1792]{1,0:T(8,128)}, f32[96,1792]{1,0:T(8,128)}, u32[]{:S(2)}, u32[]{:S(2)}) collective-permute-start(f32[96,1792]{1,0:T(8,128)} %get-tuple-element.28), channel_id=1, source_target_pairs={{1,0},{2,1},{3,2},{4,3},{5,4},{6,5},{7,6},{8,7},{9,8},{10,9},{11,1... | collective-permute-start | bytes 2064392 | tf_op jit(solution)/shard_map/ppermute | solution.py:19
  346.0 6.2 %copy-start.10 = (bf16[128,896]{1,0:T(8,128)(2,1)S(1)}, bf16[128,896]{1,0:T(8,128)(2,1)}, u32[]{:S(2)}) copy-start(bf16[128,896]{1,0:T(8,128)(2,1)} %copy.30) | copy-start | bytes 688132
  352.2 6.7 %copy-start.4 = (bf16[1,128,1792]{2,1,0:T(8,128)(2,1)S(1)}, bf16[1,128,1792]{2,1,0:T(8,128)(2,1)}, u32[]{:S(2)}) copy-start(bf16[1,128,1792]{2,1,0:T(8,128)(2,1)} %param.19) | copy-start | bytes 1376260
  361.9 5.3 %copy-start.2 = (bf16[320,8,112]{2,1,0:T(8,128)(2,1)S(1)}, bf16[320,8,112]{2,1,0:T(8,128)(2,1)}, u32[]{:S(2)}) copy-start(bf16[320,8,112]{2,1,0:T(8,128)(2,1)} %copy-done.1) | copy-start | bytes 1720324
  361.9 5.3 %copy-start.9 = (bf16[128,896]{0,1:T(8,128)(2,1)S(1)}, bf16[128,896]{0,1:T(8,128)(2,1)}, u32[]{:S(2)}) copy-start(bf16[128,896]{0,1:T(8,128)(2,1)} %copy.22) | copy-start | bytes 688132
  361.9 27.8 %all-to-all-start.2 = ((bf16[32,6,1792]{2,1,0:T(8,128)(2,1)}), bf16[32,6,1792]{2,1,0:T(8,128)(2,1)S(1)}, u32[]{:S(2)}, u32[]{:S(2)}) async-start(bf16[32,6,1792]{2,1,0:T(8,128)(2,1)} %reshape.270), calls=%async_computation.2 | async-start | bytes 1835008 | tf_op jit(solution)/shard_map/all_to_all | solution.py:143
Sparse Core Ops, SparseCore 0:
  65.2 85.6 all-gather.1
